TPU v7x, 32 devices: a whole 2x2x4 slice. The times are simulated.
32 devices in a mesh: seq: 16 (over z, y, core), dp: 2 (over x).
Axes of the slice: x: 2, y: 2, z: 4, core: 2. Of those that a mesh axis runs over, the one named last changes fastest.
Arguments:
- query_rows: bfloat16 [2, 4096, 768], P('dp', 'seq'), may hold values from -40 to 40
- key_rows: bfloat16 [2, 4096, 768], P('dp', 'seq'), may hold values from -40 to 40
- value_rows: bfloat16 [2, 4096, 768], P('dp', 'seq'), may hold values from -6 to 6
- out_grad: bfloat16 [2, 4096, 1536], P('dp', 'seq'), may hold values from -6 to 6
- lengths: int32 [2, 8], P('dp'), may hold values from 1 to 1024, 4096 in all within a row
- out_weight: bfloat16 [768, 1536], P('seq', 'dp'), may hold values from -0.21875 to 0.21875
Outputs:
- mixed_out: bfloat16 [2, 4096, 1536], P('dp', 'seq')
- query_grad: bfloat16 [2, 4096, 768], P('dp', 'seq')
- key_grad: bfloat16 [2, 4096, 768], P('dp', 'seq')
- value_grad: bfloat16 [2, 4096, 768], P('dp', 'seq')
- weight_grad: float32 [768, 1536], P('seq', 'dp')
Inputs may be any that keep to these rules, and one draw needn't show every extreme that they name: Each row holds the lengths of the 8 utterances of one group in packing order; they sum to 4096 and the longest is exactly 1024.
All inputs are finite; a program needn't handle non-finite values.
Results may differ from a plain program's by a relative error of at most 0.022.
Values may be sent and summed in bfloat16 or wider, within the bound.
No kernel may reach another device: no remote copies, remote signals or barrier semaphores. Data moves between devices by JAX's collectives and lax.ppermute only.
A program may use at most 64 MiB of HBM per device.

v0:
```python
import jax
import jax.numpy as jnp
from jax import lax
from jax.sharding import PartitionSpec as P

HEADS = 12
HEAD_DIM = 64
STRETCH = 128
MOST = 1024
MASKED_SCORE = -1e30


def shift_up(block, axis, distance):
    devices = range(lax.axis_size(axis))
    route = [(i - distance, i) for i in devices if i - distance in devices]
    return lax.ppermute(block, axis, route)


def frame_labels(utt_lengths, first_frame, frame_count, total_frames):
    positions = first_frame + jnp.arange(frame_count, dtype=jnp.int32)
    utt_ends = jnp.cumsum(utt_lengths)
    utt_index = jnp.sum((positions[:, None] >= utt_ends[None, :]).astype(jnp.int32), axis=1)
    outside = (positions < 0) | (positions >= total_frames)
    return (jnp.where(outside, -1, utt_index), positions // STRETCH)


def local(query_rows, key_rows, value_rows, out_grad, lengths, out_weight):
    seq_count = lax.axis_size("seq")
    device = lax.axis_index("seq")
    tok_rows = query_rows.shape[1]
    feature_width = query_rows.shape[2]
    total_frames = seq_count * tok_rows
    reach = min(-(-MOST // tok_rows), seq_count - 1)
    window = (reach + 1) * tok_rows
    score_scale = HEAD_DIM ** (-0.5)
    utt_lengths = lengths[0]
    weight_cols = lax.all_gather(out_weight, "dp", axis=1, tiled=True)
    weight_full = lax.all_gather(weight_cols, "seq", axis=0, tiled=True)
    query_heads = query_rows[0].reshape(tok_rows, HEADS, HEAD_DIM)
    key_value = jnp.concatenate([key_rows[0], value_rows[0]], axis=1)
    held = [key_value]
    for _ in range(reach):
        held.append(shift_up(held[-1], "seq", 1))
    kv_window = jnp.concatenate(held[::-1], axis=0)
    key_window = kv_window[:, :feature_width].reshape(window, HEADS, HEAD_DIM)
    value_window = kv_window[:, feature_width:].reshape(window, HEADS, HEAD_DIM)
    query_utt, query_stretch = frame_labels(utt_lengths, device * tok_rows, tok_rows, total_frames)
    key_utt, key_stretch = frame_labels(
        utt_lengths, (device - reach) * tok_rows, window, total_frames
    )
    visible = (query_utt[:, None] == key_utt[None, :]) & (
        key_stretch[None, :] <= query_stretch[:, None]
    )
    scores = (
        jnp.einsum("qhe,khe->hqk", query_heads, key_window, preferred_element_type=jnp.float32)
        * score_scale
    )
    masked = jnp.where(visible[None], scores, MASKED_SCORE)
    top_score = jnp.max(masked, axis=2)
    expo_full = jnp.where(visible[None], jnp.exp(masked - top_score[:, :, None]), 0.0)
    row_sum = jnp.sum(expo_full, axis=2)
    weighted = jnp.einsum(
        "hqk,khe->qhe",
        expo_full.astype(jnp.bfloat16),
        value_window,
        preferred_element_type=jnp.float32,
    )
    attended = (
        (weighted / jnp.transpose(row_sum)[:, :, None])
        .reshape(tok_rows, feature_width)
        .astype(jnp.bfloat16)
    )
    log_sum = top_score + jnp.log(row_sum)
    mixed_out = jnp.dot(attended, weight_full, preferred_element_type=jnp.float32).astype(
        jnp.bfloat16
    )
    upstream = out_grad[0]
    att_grad = lax.dot_general(
        upstream, weight_full, (((1,), (1,)), ((), ())), preferred_element_type=jnp.float32
    ).astype(jnp.bfloat16)
    partial_weight = lax.dot_general(
        attended, upstream, (((0,), (0,)), ((), ())), preferred_element_type=jnp.float32
    )
    col_share = lax.psum_scatter(partial_weight, "dp", scatter_dimension=1, tiled=True)
    weight_grad = lax.psum_scatter(col_share, "seq", scatter_dimension=0, tiled=True)
    grad_heads = att_grad.reshape(tok_rows, HEADS, HEAD_DIM)
    delta_rows = jnp.sum(
        grad_heads.astype(jnp.float32)
        * attended.reshape(tok_rows, HEADS, HEAD_DIM).astype(jnp.float32),
        axis=2,
    )
    query_acc = jnp.zeros((tok_rows, HEADS, HEAD_DIM), jnp.float32)
    carried = None
    for back in range(reach, -1, -1):
        rows = slice((reach - back) * tok_rows, (reach - back + 1) * tok_rows)
        key_block = key_window[rows]
        value_block = value_window[rows]
        block_visible = visible[:, rows]
        block_scores = (
            jnp.einsum("qhe,khe->hqk", query_heads, key_block, preferred_element_type=jnp.float32)
            * score_scale
        )
        prob_full = jnp.where(block_visible[None], jnp.exp(block_scores - log_sum[:, :, None]), 0.0)
        prob_back = prob_full.astype(jnp.bfloat16)
        prob_grad = jnp.einsum(
            "qhe,khe->hqk", grad_heads, value_block, preferred_element_type=jnp.float32
        )
        score_grad = (prob_full * (prob_grad - jnp.transpose(delta_rows)[:, :, None])).astype(
            jnp.bfloat16
        )
        query_acc = query_acc + jnp.einsum(
            "hqk,khe->qhe", score_grad, key_block, preferred_element_type=jnp.float32
        )
        key_part = (
            jnp.einsum("hqk,qhe->khe", score_grad, query_heads, preferred_element_type=jnp.float32)
            * score_scale
        )
        value_part = jnp.einsum(
            "hqk,qhe->khe", prob_back, grad_heads, preferred_element_type=jnp.float32
        )
        part = jnp.concatenate(
            [
                key_part.reshape(tok_rows, feature_width),
                value_part.reshape(tok_rows, feature_width),
            ],
            axis=1,
        )
        if carried is None:
            carried = part
        else:
            carried = shift_up(carried, "seq", -1) + part
    query_grad = (query_acc * score_scale).reshape(tok_rows, feature_width).astype(jnp.bfloat16)
    key_grad = carried[:, :feature_width].astype(jnp.bfloat16)
    value_grad = carried[:, feature_width:].astype(jnp.bfloat16)
    return (mixed_out[None], query_grad[None], key_grad[None], value_grad[None], weight_grad)


def solution(mesh):
    return jax.shard_map(
        local,
        mesh=mesh,
        in_specs=(
            P("dp", "seq", None),
            P("dp", "seq", None),
            P("dp", "seq", None),
            P("dp", "seq", None),
            P("dp", None),
            P("seq", "dp"),
        ),
        out_specs=(
            P("dp", "seq", None),
            P("dp", "seq", None),
            P("dp", "seq", None),
            P("dp", "seq", None),
            P("seq", "dp"),
        ),
        check_vma=False,
    )
```

profile of v0, /device:TPU:0, one launch (start us, length us, event | category | flops | bytes accessed | tf_op | source)
XLA Modules:
  0.0 278.8 jit_solution(4228232559934887295)
XLA Ops:
  8.5 2.4 collective-permute-start
  12.7 11.6 %collective-permute-start.1 = (bf16[256,1536]{1,0:T(8,128)(2,1)S(1)}, bf16[256,1536]{1,0:T(8,128)(2,1)S(1)}, u32[]{:S(2)}, u32[]{:S(2)}) collective-permute-start(bf16[256,1536]{1,0:T(8,128)(2,1)S(1)} %collective-permute-done), channel_id=1, source_target_pairs={{0,2},{2,4},{4,6},{6,8},{8,10},{10,12},{12,14},{14,16},{16,18},{18... | collective-permute-start | bytes 2359304 | tf_op jit(solution)/shard_map/ppermute | solution.py:16
  26.2 11.4 %collective-permute-start.2 = (bf16[256,1536]{1,0:T(8,128)(2,1)S(1)}, bf16[256,1536]{1,0:T(8,128)(2,1)S(1)}, u32[]{:S(2)}, u32[]{:S(2)}) collective-permute-start(bf16[256,1536]{1,0:T(8,128)(2,1)S(1)} %collective-permute-done.1), channel_id=1, source_target_pairs={{0,2},{2,4},{4,6},{6,8},{8,10},{10,12},{12,14},{14,16},{16,18},{18... | collective-permute-start | bytes 2359304 | tf_op jit(solution)/shard_map/ppermute | solution.py:16
  37.6 6.3 %all_gather.6 = bf16[48,1536]{1,0:T(8,128)(2,1)} all-gather(bf16[48,768]{1,0:T(8,128)(2,1)} %param.11), channel_id=1, replica_groups=mesh['seq'=16,'dp'=2] {'dp'}, dimensions={1}, use_global_device_ids=true | all-gather | bytes 221184 | tf_op jit(solution)/shard_map/all_gather | solution.py:37
  45.0 6.8 %collective-permute-start.3 = (bf16[256,1536]{1,0:T(8,128)(2,1)S(1)}, bf16[256,1536]{1,0:T(8,128)(2,1)}, u32[]{:S(2)}, u32[]{:S(2)}) collective-permute-start(bf16[256,1536]{1,0:T(8,128)(2,1)S(1)} %collective-permute-done.2), channel_id=1, source_target_pairs={{0,2},{2,4},{4,6},{6,8},{8,10},{10,12},{12,14},{14,16},{16,18},{18... | collective-permute-start | bytes 2359304 | tf_op jit(solution)/shard_map/ppermute | solution.py:16
  57.1 4.0 %copy.117 = bf16[1280,768]{0,1:T(8,128)(2,1)} copy(bf16[1280,768]{1,0:T(8,128)(2,1)} %get-tuple-element.20) | data formatting | bytes 3932160 | tf_op jit(solution)/shard_map/slice | solution.py:45
  63.4 9.6 %fusion = (f32[12,256]{1,0:T(8,128)S(1)}, f32[12,1280,256]{2,1,0:T(8,128)}) fusion(pred[256,1280]{0,1:T(8,128)(4,1)S(1)} %compare_and_fusion, bf16[1280,12,64]{0,2,1:T(8,128)(2,1)} %bitcast.189, bf16[256,12,64]{0,2,1:T(8,128)(2,1)S(1)} %bitcast.178), kind=kOutput, calls=%fused_computation.2 | convolution fusion | flops 515109888 | bytes 18427904 | tf_op jit(solution)/shard_map/qhe,khe->hqk/dot_general | solution.py:55
  73.0 9.2 %fusion.1 = f32[12,256]{1,0:T(8,128)S(1)} fusion(f32[12,1280,256]{2,1,0:T(8,128)} %get-tuple-element.38, f32[12,256]{1,0:T(8,128)S(1)} %get-tuple-element.37, pred[256,1280]{0,1:T(8,128)(4,1)S(1)} %compare_and_fusion), kind=kLoop, calls=%fused_computation.3 | loop fusion | flops 19657728 | bytes 16080896 | tf_op jit(solution)/shard_map/reduce_sum | solution.py:61
  82.2 7.5 %all-gather.2.cloned.1.call-done = bf16[768,1536]{1,0:T(8,128)(2,1)} async-done(((bf16[48,1536]{1,0:T(8,128)(2,1)}), bf16[768,1536]{1,0:T(8,128)(2,1)}) %all-gather.2.cloned.1.call-update) | async-done | bytes 2359312 | tf_op jit(solution)/shard_map/all_gather | solution.py:38
  89.7 2.5 convolution_convert_fusion.1
  92.3 10.0 %multiply_reduce_fusion = (f32[256,12]{0,1:T(8,128)S(1)}, bf16[256,12,64]{0,2,1:T(8,128)(2,1)S(1)}) fusion(bf16[256,12,64]{0,2,1:T(8,128)(2,1)S(1)} %bitcast.194, f32[256,12]{0,1:T(8,128)S(1)} %bitcast.234, bf16[1280,12,64]{0,2,1:T(8,128)(2,1)} %bitcast.223, f32[12,1280,256]{2,1,0:T(8,128)} %get-tuple-element.38, f32[12,256]{1,0:T(8,128)S(1)} %get-tuple-element.37, ...), kind=kOutput, calls=%fused_computation.75 | convolution fusion | flops 524153856 | bytes 18845696 | tf_op jit(solution)/shard_map/hqk,khe->qhe/dot_general | solution.py:62
  103.0 2.9 %fusion.54 = f32[768,1536]{1,0:T(8,128)} fusion(bf16[256,768]{0,1:T(8,128)(2,1)S(1)} %bitcast.221, bf16[1,256,1536]{2,1,0:T(8,128)(2,1)S(1)} %copy-done), kind=kOutput, calls=%fused_computation.72 | convolution fusion | flops 603979776 | bytes 5898240 | tf_op jit(solution)/shard_map/dot_general | solution.py:81
  114.1 2.3 fusion.84
  121.8 3.5 %fusion.17 = f32[12,64,256]{2,1,0:T(8,128)} fusion(bf16[256,12,64]{0,2,1:T(8,128)(2,1)S(1)} %bitcast.196, f32[12,256,256]{2,1,0:T(8,128)} %copy-done.27, f32[12,256]{1,0:T(8,128)S(1)} %log_add_fusion, pred[256,256]{0,1:T(8,128)(4,1)} %copy-done.37), kind=kOutput, calls=%fused_computation.27 | convolution fusion | flops 103809024 | bytes 4403200 | tf_op jit(solution)/shard_map/hqk,qhe->khe/dot_general | solution.py:118
  125.3 2.4 copy.145
  127.7 2.5 pad_maximum_fusion
  137.2 2.4 copy.148
  139.5 3.5 %fusion.15 = f32[12,64,256]{2,1,0:T(8,128)} fusion(bf16[256,12,64]{0,2,1:T(8,128)(2,1)S(1)} %bitcast.198, f32[12,256,256]{2,1,0:T(8,128)} %copy-done.28, f32[12,256]{1,0:T(8,128)S(1)} %log_add_fusion, pred[256,256]{0,1:T(8,128)(4,1)} %get-tuple-element.36), kind=kOutput, calls=%fused_computation.26 | convolution fusion | flops 103809024 | bytes 4403200 | tf_op jit(solution)/shard_map/hqk,qhe->khe/dot_general | solution.py:118
  143.0 2.5 copy.149
  145.4 3.3 %maximum_add_fusion = f32[256,1536]{1,0:T(8,128)} fusion(f32[256,1536]{1,0:T(8,128)} %collective-permute-done.4, f32[256,768]{1,0:T(8,128)} %copy.149, f32[256,768]{1,0:T(8,128)} %copy.148), kind=kLoop, calls=%fused_computation.30 | loop fusion | flops 786432 | bytes 4718592 | tf_op jit(solution)/shard_map/add | solution.py:131
  150.3 2.4 subtract_exponential_fusion
  152.7 3.6 %copy.138 = f32[12,256,256]{1,2,0:T(8,128)} copy(f32[12,256,256]{2,1,0:T(8,128)} %subtract_exponential_fusion) | data formatting | bytes 6291456 | tf_op jit(solution)/shard_map/exp | solution.py:103
  156.3 3.0 %multiply_convert_fusion.2 = bf16[12,256,256]{1,2,0:T(8,128)(2,1)S(1)} fusion(f32[12,256,256]{2,1,0:T(8,128)} %fusion.84, bf16[256,12,64]{0,2,1:T(8,128)(2,1)S(1)} %bitcast.199, bf16[256,12,64]{0,2,1:T(8,128)(2,1)} %bitcast.231, f32[12,256]{1,0:T(8,128)} %bitcast.237, f32[12,256]{1,0:T(8,128)S(1)} %log_add_fusion, pred[256,256]{0,1:T(8,128)(4,1)} %get-tuple-element.35), kind=kOutput, calls=%fused_computation.14 | convolution fusion | flops 105381888 | bytes 5595136 | tf_op jit(solution)/shard_map/qhe,khe->hqk/dot_general | solution.py:105
  162.0 2.3 copy.152
  164.3 3.5 %fusion.13 = f32[12,64,256]{2,1,0:T(8,128)} fusion(bf16[256,12,64]{0,2,1:T(8,128)(2,1)S(1)} %bitcast.200, f32[12,256,256]{2,1,0:T(8,128)} %fusion.84, f32[12,256]{1,0:T(8,128)S(1)} %log_add_fusion, pred[256,256]{0,1:T(8,128)(4,1)} %get-tuple-element.35), kind=kOutput, calls=%fused_computation.25 | convolution fusion | flops 103809024 | bytes 4403200 | tf_op jit(solution)/shard_map/hqk,qhe->khe/dot_general | solution.py:118
  170.1 3.5 %fusion.19 = f32[12,64,256]{2,1,0:T(8,128)} fusion(bf16[256,12,64]{0,2,1:T(8,128)(2,1)S(1)} %bitcast.201, f32[12,256,256]{1,2,0:T(8,128)} %copy.138, pred[256,256]{0,1:T(8,128)(4,1)} %get-tuple-element.33), kind=kOutput, calls=%fused_computation.28 | convolution fusion | flops 101449728 | bytes 4390912 | tf_op jit(solution)/shard_map/hqk,qhe->khe/dot_general | solution.py:118
  173.6 3.0 %maximum_add_fusion.1 = f32[256,1536]{1,0:T(8,128)} fusion(f32[256,1536]{1,0:T(8,128)} %collective-permute-done.5, f32[256,768]{1,0:T(8,128)S(1)} %copy-done.18, f32[256,768]{1,0:T(8,128)S(1)} %copy-done.17), kind=kLoop, calls=%fused_computation.31 | loop fusion | flops 786432 | bytes 4718592 | tf_op jit(solution)/shard_map/add | solution.py:131
  188.2 2.8 multiply_convert_fusion
  192.8 2.8 maximum_add_fusion.2
  208.6 3.5 %fusion.6 = bf16[1,256,1536]{2,1,0:T(8,128)(2,1)} fusion(bf16[256,768]{0,1:T(8,128)(2,1)S(1)} %bitcast.222, bf16[768,1536]{1,0:T(8,128)(2,1)} %all-gather.2.cloned.1.call-done), kind=kOutput, calls=%fused_computation.19 | convolution fusion | flops 604372992 | bytes 3538944 | tf_op jit(solution)/shard_map/dot_general | solution.py:74
  212.1 5.5 %collective-permute-done.7 = f32[256,1536]{1,0:T(8,128)} collective-permute-done((f32[256,1536]{1,0:T(8,128)}, f32[256,1536]{1,0:T(8,128)}, u32[]{:S(2)}, u32[]{:S(2)}) %collective-permute-start.7) | collective-permute-done | bytes 1572896 | tf_op jit(solution)/shard_map/ppermute | solution.py:16
  220.2 52.1 %reduce-scatter.5.cloned.1.call-done = f32[48,768]{1,0:T(8,128)} async-done(((f32[768,768]{1,0:T(8,128)}), f32[48,768]{1,0:T(8,128)}) %reduce-scatter.5.cloned.1.call-update) | async-done | bytes 147472 | tf_op jit(solution)/shard_map/reduce_scatter | solution.py:85
  (160 shorter events, 70.1 us)
Async XLA Ops:
  7.2 82.5 %copy-start = (bf16[1,256,1536]{2,1,0:T(8,128)(2,1)S(1)}, bf16[1,256,1536]{2,1,0:T(8,128)(2,1)}, u32[]{:S(2)}) copy-start(bf16[1,256,1536]{2,1,0:T(8,128)(2,1)} %param.9) | copy-start | bytes 2359300
  7.2 82.5 %all-gather.2.cloned.1.call-start = ((), (), s32[]{:S(2)}) async-start(), calls=%async_computation.2 | async-start | bytes 2506752 | tf_op jit(solution)/shard_map/all_gather | solution.py:38
  8.5 4.3 %collective-permute-start = (bf16[256,1536]{1,0:T(8,128)(2,1)S(1)}, bf16[256,1536]{1,0:T(8,128)(2,1)S(1)}, u32[]{:S(2)}, u32[]{:S(2)}) collective-permute-start(bf16[256,1536]{1,0:T(8,128)(2,1)S(1)} %pad_maximum_fusion.1), channel_id=1, source_target_pairs={{0,2},{2,4},{4,6},{6,8},{8,10},{10,12},{12,14},{14,16},{16,18},{18... | collective-permute-start | bytes 2359304 | tf_op jit(solution)/shard_map/ppermute | solution.py:16
  12.7 13.5 %copy-start.23 = (bf16[256,1536]{1,0:T(8,128)(2,1)}, bf16[256,1536]{1,0:T(8,128)(2,1)S(1)}, u32[]{:S(2)}) copy-start(bf16[256,1536]{1,0:T(8,128)(2,1)S(1)} %collective-permute-done) | copy-start | bytes 2359300
  12.7 13.4 %collective-permute-start.1 = (bf16[256,1536]{1,0:T(8,128)(2,1)S(1)}, bf16[256,1536]{1,0:T(8,128)(2,1)S(1)}, u32[]{:S(2)}, u32[]{:S(2)}) collective-permute-start(bf16[256,1536]{1,0:T(8,128)(2,1)S(1)} %collective-permute-done), channel_id=1, source_target_pairs={{0,2},{2,4},{4,6},{6,8},{8,10},{10,12},{12,14},{14,16},{16,18},{18... | collective-permute-start | bytes 2359304 | tf_op jit(solution)/shard_map/ppermute | solution.py:16
  26.2 29.2 %copy-start.21 = (bf16[256,1536]{1,0:T(8,128)(2,1)}, bf16[256,1536]{1,0:T(8,128)(2,1)S(1)}, u32[]{:S(2)}) copy-start(bf16[256,1536]{1,0:T(8,128)(2,1)S(1)} %collective-permute-done.1) | copy-start | bytes 2359300
  26.2 18.8 %collective-permute-start.2 = (bf16[256,1536]{1,0:T(8,128)(2,1)S(1)}, bf16[256,1536]{1,0:T(8,128)(2,1)S(1)}, u32[]{:S(2)}, u32[]{:S(2)}) collective-permute-start(bf16[256,1536]{1,0:T(8,128)(2,1)S(1)} %collective-permute-done.1), channel_id=1, source_target_pairs={{0,2},{2,4},{4,6},{6,8},{8,10},{10,12},{12,14},{14,16},{16,18},{18... | collective-permute-start | bytes 2359304 | tf_op jit(solution)/shard_map/ppermute | solution.py:16
  44.0 138.1 %reduce-scatter.3.cloned.1.call-start = ((), (), s32[]{:S(2)}) async-start(), calls=%async_computation.3 | async-start | bytes 7077888 | tf_op jit(solution)/shard_map/reduce_scatter | solution.py:84
  45.0 10.5 %copy-start.19 = (bf16[256,1536]{1,0:T(8,128)(2,1)}, bf16[256,1536]{1,0:T(8,128)(2,1)S(1)}, u32[]{:S(2)}) copy-start(bf16[256,1536]{1,0:T(8,128)(2,1)S(1)} %collective-permute-done.2) | copy-start | bytes 2359300
  45.0 9.0 %collective-permute-start.3 = (bf16[256,1536]{1,0:T(8,128)(2,1)S(1)}, bf16[256,1536]{1,0:T(8,128)(2,1)}, u32[]{:S(2)}, u32[]{:S(2)}) collective-permute-start(bf16[256,1536]{1,0:T(8,128)(2,1)S(1)} %collective-permute-done.2), channel_id=1, source_target_pairs={{0,2},{2,4},{4,6},{6,8},{8,10},{10,12},{12,14},{14,16},{16,18},{18... | collective-permute-start | bytes 2359304 | tf_op jit(solution)/shard_map/ppermute | solution.py:16
  102.3 16.3 %copy-start.38 = (f32[256,12]{0,1:T(8,128)}, f32[256,12]{0,1:T(8,128)S(1)}, u32[]{:S(2)}) copy-start(f32[256,12]{0,1:T(8,128)S(1)} %get-tuple-element.39) | copy-start | bytes 36868
  106.0 166.3 %reduce-scatter.5.cloned.1.call-start = ((), (), s32[]{:S(2)}) async-start(), calls=%async_computation.4 | async-start | bytes 2506752 | tf_op jit(solution)/shard_map/reduce_scatter | solution.py:85
  109.5 9.1 %copy-start.37 = (pred[256,256]{0,1:T(8,128)(4,1)}, pred[256,256]{0,1:T(8,128)(4,1)S(1)}, u32[]{:S(2)}) copy-start(pred[256,256]{0,1:T(8,128)(4,1)S(1)} %get-tuple-element.32) | copy-start | bytes 196612
  125.3 6.1 %copy-start.20 = (bf16[256,1536]{1,0:T(8,128)(2,1)S(1)}, bf16[256,1536]{1,0:T(8,128)(2,1)}, u32[]{:S(2)}) copy-start(bf16[256,1536]{1,0:T(8,128)(2,1)} %copy-done.19) | copy-start | bytes 2359300
  130.1 15.3 %collective-permute-start.4 = (f32[256,1536]{1,0:T(8,128)}, f32[256,1536]{1,0:T(8,128)}, u32[]{:S(2)}, u32[]{:S(2)}) collective-permute-start(f32[256,1536]{1,0:T(8,128)} %pad_maximum_fusion), channel_id=1, source_target_pairs={{2,0},{4,2},{6,4},{8,6},{10,8},{12,10},{14,12},{16,14},{18,16},{20... | collective-permute-start | bytes 4718600 | tf_op jit(solution)/shard_map/ppermute | solution.py:16
  131.7 4.0 %copy-start.11 = (bf16[256,768]{0,1:T(8,128)(2,1)}, bf16[256,768]{0,1:T(8,128)(2,1)S(1)}, u32[]{:S(2)}) copy-start(bf16[256,768]{0,1:T(8,128)(2,1)S(1)} %copy.125) | copy-start | bytes 1179652
  133.2 4.0 %copy-start.28 = (f32[12,256,256]{2,1,0:T(8,128)}, f32[12,256,256]{2,1,0:T(8,128)S(1)}, u32[]{:S(2)}) copy-start(f32[12,256,256]{2,1,0:T(8,128)S(1)} %fusion.82) | copy-start | bytes 9437188
  143.0 7.3 %copy-start.10 = (bf16[1,256,768]{1,2,0:T(8,128)(2,1)S(1)}, bf16[1,256,768]{1,2,0:T(8,128)(2,1)}, u32[]{:S(2)}) copy-start(bf16[1,256,768]{1,2,0:T(8,128)(2,1)} %copy.137) | copy-start | bytes 1179652
  148.7 24.9 %collective-permute-start.5 = (f32[256,1536]{1,0:T(8,128)}, f32[256,1536]{1,0:T(8,128)}, u32[]{:S(2)}, u32[]{:S(2)}) collective-permute-start(f32[256,1536]{1,0:T(8,128)} %maximum_add_fusion), channel_id=1, source_target_pairs={{2,0},{4,2},{6,4},{8,6},{10,8},{12,10},{14,12},{16,14},{18,16},{20... | collective-permute-start | bytes 4718600 | tf_op jit(solution)/shard_map/ppermute | solution.py:16
  173.6 4.4 %copy-start.12 = (bf16[256,768]{0,1:T(8,128)(2,1)S(1)}, bf16[256,768]{0,1:T(8,128)(2,1)}, u32[]{:S(2)}) copy-start(bf16[256,768]{0,1:T(8,128)(2,1)} %copy-done.11) | copy-start | bytes 1179652
  173.6 5.7 %copy-start.26 = (f32[12,256,256]{2,1,0:T(8,128)S(1)}, f32[12,256,256]{2,1,0:T(8,128)}, u32[]{:S(2)}) copy-start(f32[12,256,256]{2,1,0:T(8,128)} %fusion.86) | copy-start | bytes 9437188
  173.6 5.7 %copy-start.36 = (pred[256,256]{0,1:T(8,128)(4,1)S(1)}, pred[256,256]{0,1:T(8,128)(4,1)}, u32[]{:S(2)}) copy-start(pred[256,256]{0,1:T(8,128)(4,1)} %get-tuple-element.34) | copy-start | bytes 196612
  176.6 4.4 %copy-start.34 = (bf16[256,768]{0,1:T(8,128)(2,1)S(1)}, bf16[256,768]{0,1:T(8,128)(2,1)}, u32[]{:S(2)}) copy-start(bf16[256,768]{0,1:T(8,128)(2,1)} %copy.134) | copy-start | bytes 1179652
  176.6 4.4 %copy-start.39 = (f32[256,12]{0,1:T(8,128)S(1)}, f32[256,12]{0,1:T(8,128)}, u32[]{:S(2)}) copy-start(f32[256,12]{0,1:T(8,128)} %copy-done.38) | copy-start | bytes 36868
  176.6 16.2 %collective-permute-start.6 = (f32[256,1536]{1,0:T(8,128)}, f32[256,1536]{1,0:T(8,128)}, u32[]{:S(2)}, u32[]{:S(2)}) collective-permute-start(f32[256,1536]{1,0:T(8,128)} %maximum_add_fusion.1), channel_id=1, source_target_pairs={{2,0},{4,2},{6,4},{8,6},{10,8},{12,10},{14,12},{16,14},{18,16},{20... | collective-permute-start | bytes 4718600 | tf_op jit(solution)/shard_map/ppermute | solution.py:16
  182.1 6.1 %copy-start.40 = (f32[256,12]{0,1:T(8,128)S(1)}, f32[256,12]{0,1:T(8,128)}, u32[]{:S(2)}) copy-start(f32[256,12]{0,1:T(8,128)} %copy-done.38) | copy-start | bytes 36868
  188.2 4.6 %copy-start.15 = (f32[256,768]{1,0:T(8,128)S(1)}, f32[256,768]{1,0:T(8,128)}, u32[]{:S(2)}) copy-start(f32[256,768]{1,0:T(8,128)} %copy.156) | copy-start | bytes 2359300
  188.2 4.6 %copy-start.16 = (f32[256,768]{1,0:T(8,128)S(1)}, f32[256,768]{1,0:T(8,128)}, u32[]{:S(2)}) copy-start(f32[256,768]{1,0:T(8,128)} %copy.157) | copy-start | bytes 2359300
  195.5 22.1 %collective-permute-start.7 = (f32[256,1536]{1,0:T(8,128)}, f32[256,1536]{1,0:T(8,128)}, u32[]{:S(2)}, u32[]{:S(2)}) collective-permute-start(f32[256,1536]{1,0:T(8,128)} %maximum_add_fusion.2), channel_id=1, source_target_pairs={{2,0},{4,2},{6,4},{8,6},{10,8},{12,10},{14,12},{16,14},{18,16},{20... | collective-permute-start | bytes 4718600 | tf_op jit(solution)/shard_map/ppermute | solution.py:16
  207.7 10.0 %copy-start.29 = (f32[256,768]{1,0:T(8,128)S(1)}, f32[256,768]{1,0:T(8,128)}, u32[]{:S(2)}) copy-start(f32[256,768]{1,0:T(8,128)} %copy.160) | copy-start | bytes 2359300
  207.7 10.0 %copy-start.30 = (f32[256,768]{1,0:T(8,128)S(1)}, f32[256,768]{1,0:T(8,128)}, u32[]{:S(2)}) copy-start(f32[256,768]{1,0:T(8,128)} %copy.161) | copy-start | bytes 2359300
  208.6 63.7 %copy-start.1 = (bf16[1,256,1536]{2,1,0:T(8,128)(2,1)S(1)}, bf16[1,256,1536]{2,1,0:T(8,128)(2,1)}, u32[]{:S(2)}) copy-start(bf16[1,256,1536]{2,1,0:T(8,128)(2,1)} %param.9) | copy-start | bytes 2359300
  (20 other events, 43.8 us)
Sparse Core Ops, SparseCore 0:
  44.1 45.5 all-gather.1
  106.1 68.8 reduce-scatter.2
  182.3 90.0 reduce-scatter.4
where the time goes:
time: 280 us; the launch traced here: 279 us
  matrix products  74.8 us (27%)
  waiting for transfers between devices  70.7 us (25%)
  local copies, waits for them, and re-layouts  49.1 us (18%)
  starting transfers between devices  38.1 us (14%)
  other arithmetic  25.5 us (9%)
  between operations  14.4 us (5%)
  blocking collectives  6.32 us (2%)
    reduce_scatter x1, waiting for transfers between devices, local(): lax.psum_scatter(col_share, 'seq', scatter_dimension=0, tiled=True)  52.1 us
    ppermute x8, starting transfers between devices, shift_up(): return lax.ppermute(block, axis, route)  37.7 us
    dot_general x5, matrix products, local(): jnp.einsum('hqk,qhe->khe', prob_back, grad_heads, preferred_element_type=...  15.6 us
    reshape x5, local copies, waits for them, and re-layouts, local(): value_part.reshape(tok_rows, feature_width)  11.7 us
    ppermute x8, waiting for transfers between devices, shift_up(): return lax.ppermute(block, axis, route)  11 us
    dot_general x5, matrix products, local(): jnp.einsum('qhe,khe->hqk', grad_heads, value_block, preferred_element_typ...  10.1 us
    dot_general x1, matrix products, local(): jnp.einsum('hqk,khe->qhe', expo_full.astype(jnp.bfloat16), value_window,...  9.96 us
    dot_general x1, matrix products, local(): jnp.einsum('qhe,khe->hqk', query_heads, key_window, preferred_element_typ...  9.62 us
  transfers between devices with their start and end apart: 11, of which 6 were waited for; matrix products, arithmetic and copies ran while one was open for 46% of the time, Pallas kernels for 0%

commit v1 on v0

--- a/solution.py
+++ b/solution.py
@@ -8,6 +8,28 @@
 STRETCH = 128
 MOST = 1024
 MASKED_SCORE = -1e30
+
+
+def in_order(blocks, dim):
+    blocks = jnp.moveaxis(blocks, 0, dim)
+    lengths = blocks.shape
+    return blocks.reshape(*lengths[:dim], lengths[dim] * lengths[dim + 1], *lengths[dim + 2 :])
+
+
+def ring_gather(value, axis, dim):
+    devices = lax.axis_size(axis)
+    pairs = [(i, (i + 1) % devices) for i in range(devices)]
+    back = [(b, a) for a, b in pairs]
+    lower, upper = ([], [])
+    for lap in range(devices - 1):
+        if lap % 2 == 0:
+            lower.append(lax.ppermute(lower[-1] if lower else value, axis, pairs))
+        else:
+            upper.append(lax.ppermute(upper[-1] if upper else value, axis, back))
+    pieces = jnp.stack([*lower[::-1], value, *upper])
+    shift = lax.axis_index(axis) - len(lower)
+    pieces = pieces[(jnp.arange(devices) - shift) % devices]
+    return in_order(pieces, dim)
 
 
 def shift_up(block, axis, distance):
@@ -35,7 +57,7 @@
     score_scale = HEAD_DIM ** (-0.5)
     utt_lengths = lengths[0]
     weight_cols = lax.all_gather(out_weight, "dp", axis=1, tiled=True)
-    weight_full = lax.all_gather(weight_cols, "seq", axis=0, tiled=True)
+    weight_full = ring_gather(weight_cols, "seq", 0)
     query_heads = query_rows[0].reshape(tok_rows, HEADS, HEAD_DIM)
     key_value = jnp.concatenate([key_rows[0], value_rows[0]], axis=1)
     held = [key_value]

time: 280 us -> 318 us (1.14)
  local copies, waits for them, and re-layouts: 49.1 us -> 67.7 us
  waiting for transfers between devices: 70.7 us -> 85 us
  starting transfers between devices: 38.1 us -> 46.5 us
  matrix products: 74.8 us -> 70.8 us
    ppermute x0 -> x15, starting transfers between devices: none -> 32.3 us  [the longest x7 32.3 us: ring_gather(): upper.append(lax.ppermute(upper[-1] if upper else value, axis, back))]
    ppermute x8, starting transfers between devices: 37.7 us -> 13.9 us  [shift_up(): return lax.ppermute(block, axis, route)]
    unnamed x90 -> x131, local copies, waits for them, and re-layouts: 9.62 us -> 31.8 us
    ppermute x0 -> x15, waiting for transfers between devices: none -> 19 us  [the longest x8 14.7 us: ring_gather(): lower.append(lax.ppermute(lower[-1] if lower else value, axis, pairs))]
    all_gather x1 -> x0, waiting for transfers between devices: 7.5 us -> none  [local(): weight_full = lax.all_gather(weight_cols, 'seq', axis=0, tiled=True)]
    ppermute x8, waiting for transfers between devices: 11 us -> 16.2 us  [shift_up(): return lax.ppermute(block, axis, route)]
    reshape x5, local copies, waits for them, and re-layouts: 11.7 us -> 6.65 us  [local(): value_part.reshape(tok_rows, feature_width)]
    dot_general x5, matrix products: 15.6 us -> 12 us  [local(): jnp.einsum('hqk,qhe->khe', prob_back, grad_heads, preferred_element_type=...]
  transfers between devices with their start and end apart: 11 -> 25, of which waited for: 6 -> 16; matrix products, arithmetic and copies ran while one was open for 46% -> 37% of each run, Pallas kernels for 0% -> 0%
where the time goes in v1:
time: 318 us; the launch traced here: 316 us
  waiting for transfers between devices  85 us (27%)
  matrix products  70.8 us (22%)
  local copies, waits for them, and re-layouts  67.7 us (21%)
  starting transfers between devices  46.5 us (15%)
  other arithmetic  25.1 us (8%)
  between operations  14.9 us (5%)
  blocking collectives  6.33 us (2%)
    reduce_scatter x1, waiting for transfers between devices, local(): lax.psum_scatter(col_share, 'seq', scatter_dimension=0, tiled=True)  49.8 us
    ppermute x7, starting transfers between devices, ring_gather(): upper.append(lax.ppermute(upper[-1] if upper else value, axis, back))  32.3 us
    unnamed x131, local copies, waits for them, and re-layouts  31.8 us
    ppermute x8, waiting for transfers between devices, shift_up(): return lax.ppermute(block, axis, route)  16.2 us
    ppermute x8, waiting for transfers between devices, ring_gather(): lower.append(lax.ppermute(lower[-1] if lower else value, axis, pairs))  14.7 us
    ppermute x8, starting transfers between devices, shift_up(): return lax.ppermute(block, axis, route)  13.9 us
    dot_general x5, matrix products, local(): jnp.einsum('qhe,khe->hqk', grad_heads, value_block, preferred_element_typ...  13.5 us
    dot_general x5, matrix products, local(): jnp.einsum('hqk,qhe->khe', prob_back, grad_heads, preferred_element_type=...  12 us
  transfers between devices with their start and end apart: 25, of which 16 were waited for; matrix products, arithmetic and copies ran while one was open for 37% of the time, Pallas kernels for 0%

profile of v1, /device:TPU:0, one launch (start us, length us, event | category | flops | bytes accessed | tf_op | source)
XLA Modules:
  0.0 316.4 jit_solution(13960345634651462236)
XLA Ops:
  7.2 6.3 %all_gather.3 = bf16[48,1536]{1,0:T(8,128)(2,1)S(1)} all-gather(bf16[48,768]{1,0:T(8,128)(2,1)} %param.11), channel_id=1, replica_groups=mesh['seq'=16,'dp'=2] {'dp'}, dimensions={1}, use_global_device_ids=true | all-gather | bytes 221184 | tf_op jit(solution)/shard_map/all_gather | solution.py:59
  13.6 4.4 %collective-permute-start.12 = (bf16[48,1536]{1,0:T(8,128)(2,1)S(1)}, bf16[48,1536]{1,0:T(8,128)(2,1)S(1)}, u32[]{:S(2)}, u32[]{:S(2)}) collective-permute-start(bf16[48,1536]{1,0:T(8,128)(2,1)S(1)} %all_gather.3), channel_id=1, source_target_pairs={{2,0},{4,2},{6,4},{8,6},{10,8},{12,10},{14,12},{16,14},{18,16},{20... | collective-permute-start | bytes 442376 | tf_op jit(solution)/shard_map/ppermute | solution.py:28
  18.0 2.9 collective-permute-done.4
  23.5 4.7 %collective-permute-done.5 = bf16[48,1536]{1,0:T(8,128)(2,1)S(1)} collective-permute-done((bf16[48,1536]{1,0:T(8,128)(2,1)S(1)}, bf16[48,1536]{1,0:T(8,128)(2,1)S(1)}, u32[]{:S(2)}, u32[]{:S(2)}) %collective-permute-start.5) | collective-permute-done | bytes 147488 | tf_op jit(solution)/shard_map/ppermute | solution.py:26
  29.2 4.4 %collective-permute-start.13 = (bf16[48,1536]{1,0:T(8,128)(2,1)S(1)}, bf16[48,1536]{1,0:T(8,128)(2,1)S(1)}, u32[]{:S(2)}, u32[]{:S(2)}) collective-permute-start(bf16[48,1536]{1,0:T(8,128)(2,1)S(1)} %collective-permute-done.12), channel_id=1, source_target_pairs={{2,0},{4,2},{6,4},{8,6},{10,8},{12,10},{14,12},{16,14},{18,16},{20... | collective-permute-start | bytes 442376 | tf_op jit(solution)/shard_map/ppermute | solution.py:28
  37.0 4.6 %collective-permute-start.14 = (bf16[48,1536]{1,0:T(8,128)(2,1)S(1)}, bf16[48,1536]{1,0:T(8,128)(2,1)S(1)}, u32[]{:S(2)}, u32[]{:S(2)}) collective-permute-start(bf16[48,1536]{1,0:T(8,128)(2,1)S(1)} %collective-permute-done.13), channel_id=1, source_target_pairs={{2,0},{4,2},{6,4},{8,6},{10,8},{12,10},{14,12},{16,14},{18,16},{20... | collective-permute-start | bytes 442376 | tf_op jit(solution)/shard_map/ppermute | solution.py:28
  44.9 4.7 %collective-permute-start.15 = (bf16[48,1536]{1,0:T(8,128)(2,1)S(1)}, bf16[48,1536]{1,0:T(8,128)(2,1)}, u32[]{:S(2)}, u32[]{:S(2)}) collective-permute-start(bf16[48,1536]{1,0:T(8,128)(2,1)S(1)} %collective-permute-done.14), channel_id=1, source_target_pairs={{2,0},{4,2},{6,4},{8,6},{10,8},{12,10},{14,12},{16,14},{18,16},{20... | collective-permute-start | bytes 442376 | tf_op jit(solution)/shard_map/ppermute | solution.py:28
  52.3 4.7 %collective-permute-start.16 = (bf16[48,1536]{1,0:T(8,128)(2,1)}, bf16[48,1536]{1,0:T(8,128)(2,1)}, u32[]{:S(2)}, u32[]{:S(2)}) collective-permute-start(bf16[48,1536]{1,0:T(8,128)(2,1)} %collective-permute-done.15), channel_id=1, source_target_pairs={{2,0},{4,2},{6,4},{8,6},{10,8},{12,10},{14,12},{16,14},{18,16},{20... | collective-permute-start | bytes 442376 | tf_op jit(solution)/shard_map/ppermute | solution.py:28
  60.0 4.7 %collective-permute-start.17 = (bf16[48,1536]{1,0:T(8,128)(2,1)}, bf16[48,1536]{1,0:T(8,128)(2,1)}, u32[]{:S(2)}, u32[]{:S(2)}) collective-permute-start(bf16[48,1536]{1,0:T(8,128)(2,1)} %collective-permute-done.16), channel_id=1, source_target_pairs={{2,0},{4,2},{6,4},{8,6},{10,8},{12,10},{14,12},{16,14},{18,16},{20... | collective-permute-start | bytes 442376 | tf_op jit(solution)/shard_map/ppermute | solution.py:28
  67.7 4.7 %collective-permute-start.18 = (bf16[48,1536]{1,0:T(8,128)(2,1)}, bf16[48,1536]{1,0:T(8,128)(2,1)S(1)}, u32[]{:S(2)}, u32[]{:S(2)}) collective-permute-start(bf16[48,1536]{1,0:T(8,128)(2,1)} %collective-permute-done.17), channel_id=1, source_target_pairs={{2,0},{4,2},{6,4},{8,6},{10,8},{12,10},{14,12},{16,14},{18,16},{20... | collective-permute-start | bytes 442376 | tf_op jit(solution)/shard_map/ppermute | solution.py:28
  93.9 3.2 %collective-permute-start.3 = (bf16[256,1536]{1,0:T(8,128)(2,1)}, bf16[256,1536]{1,0:T(8,128)(2,1)}, u32[]{:S(2)}, u32[]{:S(2)}) collective-permute-start(bf16[256,1536]{1,0:T(8,128)(2,1)} %collective-permute-done.2), channel_id=1, source_target_pairs={{0,2},{2,4},{4,6},{6,8},{8,10},{10,12},{12,14},{14,16},{16,18},{18... | collective-permute-start | bytes 2359304 | tf_op jit(solution)/shard_map/ppermute | solution.py:38
  107.8 4.0 %copy.115 = bf16[1280,768]{0,1:T(8,128)(2,1)} copy(bf16[1280,768]{1,0:T(8,128)(2,1)} %get-tuple-element.20) | data formatting | bytes 3932160 | tf_op jit(solution)/shard_map/slice | solution.py:67
  114.0 9.5 %fusion = (f32[12,256]{1,0:T(8,128)S(1)}, f32[12,1280,256]{2,1,0:T(8,128)}) fusion(pred[256,1280]{0,1:T(8,128)(4,1)S(1)} %copy-done.8, bf16[1280,12,64]{0,2,1:T(8,128)(2,1)} %bitcast.228, bf16[256,12,64]{0,2,1:T(8,128)(2,1)S(1)} %bitcast.215), kind=kOutput, calls=%fused_computation.3 | convolution fusion | flops 515109888 | bytes 18427904 | tf_op jit(solution)/shard_map/qhe,khe->hqk/dot_general | solution.py:77
  123.6 9.3 %fusion.1 = f32[12,256]{1,0:T(8,128)S(1)} fusion(f32[12,1280,256]{2,1,0:T(8,128)} %get-tuple-element.38, f32[12,256]{1,0:T(8,128)S(1)} %get-tuple-element.37, pred[256,1280]{0,1:T(8,128)(4,1)S(1)} %copy-done.8), kind=kLoop, calls=%fused_computation.4 | loop fusion | flops 19657728 | bytes 16080896 | tf_op jit(solution)/shard_map/reduce_sum | solution.py:83
  132.9 7.7 %multiply_reduce_fusion = (f32[256,12]{0,1:T(8,128)S(1)}, bf16[256,12,64]{0,2,1:T(8,128)(2,1)S(1)}) fusion(bf16[256,12,64]{0,2,1:T(8,128)(2,1)S(1)} %bitcast.255, f32[256,12]{0,1:T(8,128)S(1)} %bitcast.273, bf16[1280,12,64]{0,2,1:T(8,128)(2,1)S(1)} %bitcast.251, f32[12,1280,256]{2,1,0:T(8,128)} %get-tuple-element.38, f32[12,256]{1,0:T(8,128)S(1)} %get-tuple-element.37, ...), kind=kOutput, calls=%fused_computation.76 | convolution fusion | flops 524153856 | bytes 18845696 | tf_op jit(solution)/shard_map/hqk,khe->qhe/dot_general | solution.py:84
  141.3 2.9 fusion.54
  159.7 3.0 multiply_convert_fusion.4
  175.0 3.1 multiply_convert_fusion.3
  182.3 2.8 maximum_add_fusion
  189.1 3.7 %copy.135 = f32[12,256,256]{1,2,0:T(8,128)} copy(f32[12,256,256]{2,1,0:T(8,128)} %subtract_exponential_fusion) | data formatting | bytes 6291456 | tf_op jit(solution)/shard_map/exp | solution.py:125
  192.7 2.6 fusion.13
  196.5 3.2 %multiply_convert_fusion.2 = bf16[12,256,256]{1,2,0:T(8,128)(2,1)S(1)} fusion(f32[12,256,256]{2,1,0:T(8,128)} %fusion.86, bf16[256,12,64]{0,2,1:T(8,128)(2,1)} %bitcast.252, bf16[256,12,64]{0,2,1:T(8,128)(2,1)} %bitcast.270, f32[12,256]{1,0:T(8,128)} %bitcast.276, f32[12,256]{1,0:T(8,128)S(1)} %log_add_fusion, pred[256,256]{0,1:T(8,128)(4,1)} %get-tuple-element.35), kind=kOutput, calls=%fused_computation.15 | convolution fusion | flops 105381888 | bytes 5595136 | tf_op jit(solution)/shard_map/qhe,khe->hqk/dot_general | solution.py:127
  203.6 3.6 %fusion.11 = f32[12,64,256]{2,1,0:T(8,128)} fusion(bf16[256,12,64]{0,2,1:T(8,128)(2,1)} %bitcast.253, f32[12,256,256]{2,1,0:T(8,128)} %fusion.88, f32[12,256]{1,0:T(8,128)S(1)} %log_add_fusion, pred[256,256]{0,1:T(8,128)(4,1)} %get-tuple-element.34), kind=kOutput, calls=%fused_computation.25 | convolution fusion | flops 103809024 | bytes 4403200 | tf_op jit(solution)/shard_map/hqk,qhe->khe/dot_general | solution.py:140
  209.5 3.3 %maximum_add_fusion.1 = f32[256,1536]{1,0:T(8,128)} fusion(f32[256,1536]{1,0:T(8,128)} %collective-permute-done.20, f32[256,768]{1,0:T(8,128)} %copy.150, f32[256,768]{1,0:T(8,128)} %copy.149), kind=kLoop, calls=%fused_computation.32 | loop fusion | flops 786432 | bytes 4718592 | tf_op jit(solution)/shard_map/add | solution.py:153
  220.2 2.7 fusion.89
  224.2 3.0 multiply_convert_fusion
  227.2 4.9 %collective-permute-done.21 = f32[256,1536]{1,0:T(8,128)} collective-permute-done((f32[256,1536]{1,0:T(8,128)}, f32[256,1536]{1,0:T(8,128)}, u32[]{:S(2)}, u32[]{:S(2)}) %collective-permute-start.21) | collective-permute-done | bytes 1572896 | tf_op jit(solution)/shard_map/ppermute | solution.py:38
  232.1 2.8 maximum_add_fusion.2
  238.7 2.5 fusion.19
  242.3 3.5 %fusion.6 = bf16[1,256,1536]{2,1,0:T(8,128)(2,1)} fusion(bf16[256,768]{0,1:T(8,128)(2,1)} %bitcast.250, bf16[768,1536]{1,0:T(8,128)(2,1)} %bitcast.227), kind=kOutput, calls=%fused_computation.20 | convolution fusion | flops 604372992 | bytes 3538944 | tf_op jit(solution)/shard_map/dot_general | solution.py:96
  245.9 11.4 %collective-permute-done.22 = f32[256,1536]{1,0:T(8,128)} collective-permute-done((f32[256,1536]{1,0:T(8,128)}, f32[256,1536]{1,0:T(8,128)}, u32[]{:S(2)}, u32[]{:S(2)}) %collective-permute-start.22) | collective-permute-done | bytes 1572896 | tf_op jit(solution)/shard_map/ppermute | solution.py:38
  259.7 49.8 %reduce-scatter.5.cloned.1.call-done = f32[48,768]{1,0:T(8,128)} async-done(((f32[768,768]{1,0:T(8,128)}), f32[48,768]{1,0:T(8,128)}) %reduce-scatter.5.cloned.1.call-update) | async-done | bytes 147472 | tf_op jit(solution)/shard_map/reduce_scatter | solution.py:107
  (231 shorter events, 112.8 us)
Async XLA Ops:
  7.2 94.6 %copy-start = (bf16[1,256,1536]{2,1,0:T(8,128)(2,1)S(1)}, bf16[1,256,1536]{2,1,0:T(8,128)(2,1)}, u32[]{:S(2)}) copy-start(bf16[1,256,1536]{2,1,0:T(8,128)(2,1)} %param.9) | copy-start | bytes 2359300
  7.2 58.4 %copy-start.37 = (bf16[1,256,768]{2,1,0:T(8,128)(2,1)S(1)}, bf16[1,256,768]{2,1,0:T(8,128)(2,1)}, u32[]{:S(2)}) copy-start(bf16[1,256,768]{2,1,0:T(8,128)(2,1)} %param.6) | copy-start | bytes 1179652
  7.2 217.0 %reduce-scatter.3.cloned.1.call-start = ((), (), s32[]{:S(2)}) async-start(), calls=%async_computation.2 | async-start | bytes 7077888 | tf_op jit(solution)/shard_map/reduce_scatter | solution.py:106
  13.6 7.4 %collective-permute-start.4 = (bf16[48,1536]{1,0:T(8,128)(2,1)S(1)}, bf16[48,1536]{1,0:T(8,128)(2,1)S(1)}, u32[]{:S(2)}, u32[]{:S(2)}) collective-permute-start(bf16[48,1536]{1,0:T(8,128)(2,1)S(1)} %all_gather.3), channel_id=1, source_target_pairs={{0,2},{2,4},{4,6},{6,8},{8,10},{10,12},{12,14},{14,16},{16,18},{18... | collective-permute-start | bytes 442376 | tf_op jit(solution)/shard_map/ppermute | solution.py:26
  13.6 15.6 %collective-permute-start.12 = (bf16[48,1536]{1,0:T(8,128)(2,1)S(1)}, bf16[48,1536]{1,0:T(8,128)(2,1)S(1)}, u32[]{:S(2)}, u32[]{:S(2)}) collective-permute-start(bf16[48,1536]{1,0:T(8,128)(2,1)S(1)} %all_gather.3), channel_id=1, source_target_pairs={{2,0},{4,2},{6,4},{8,6},{10,8},{12,10},{14,12},{16,14},{18,16},{20... | collective-permute-start | bytes 442376 | tf_op jit(solution)/shard_map/ppermute | solution.py:28
  20.9 44.7 %copy-start.39 = (bf16[48,1536]{1,0:T(8,128)(2,1)}, bf16[48,1536]{1,0:T(8,128)(2,1)S(1)}, u32[]{:S(2)}) copy-start(bf16[48,1536]{1,0:T(8,128)(2,1)S(1)} %collective-permute-done.4) | copy-start | bytes 442372
  20.9 7.3 %collective-permute-start.5 = (bf16[48,1536]{1,0:T(8,128)(2,1)S(1)}, bf16[48,1536]{1,0:T(8,128)(2,1)S(1)}, u32[]{:S(2)}, u32[]{:S(2)}) collective-permute-start(bf16[48,1536]{1,0:T(8,128)(2,1)S(1)} %collective-permute-done.4), channel_id=1, source_target_pairs={{0,2},{2,4},{4,6},{6,8},{8,10},{10,12},{12,14},{14,16},{16,18},{18... | collective-permute-start | bytes 442376 | tf_op jit(solution)/shard_map/ppermute | solution.py:26
  22.2 43.7 %collective-permute-start = (bf16[256,1536]{1,0:T(8,128)(2,1)S(1)}, bf16[256,1536]{1,0:T(8,128)(2,1)S(1)}, u32[]{:S(2)}, u32[]{:S(2)}) collective-permute-start(bf16[256,1536]{1,0:T(8,128)(2,1)S(1)} %pad_maximum_fusion.1), channel_id=1, source_target_pairs={{0,2},{2,4},{4,6},{6,8},{8,10},{10,12},{12,14},{14,16},{16,18},{18... | collective-permute-start | bytes 2359304 | tf_op jit(solution)/shard_map/ppermute | solution.py:38
  28.2 37.4 %copy-start.40 = (bf16[48,1536]{1,0:T(8,128)(2,1)}, bf16[48,1536]{1,0:T(8,128)(2,1)S(1)}, u32[]{:S(2)}) copy-start(bf16[48,1536]{1,0:T(8,128)(2,1)S(1)} %collective-permute-done.5) | copy-start | bytes 442372
  28.2 7.4 %collective-permute-start.6 = (bf16[48,1536]{1,0:T(8,128)(2,1)S(1)}, bf16[48,1536]{1,0:T(8,128)(2,1)}, u32[]{:S(2)}, u32[]{:S(2)}) collective-permute-start(bf16[48,1536]{1,0:T(8,128)(2,1)S(1)} %collective-permute-done.5), channel_id=1, source_target_pairs={{0,2},{2,4},{4,6},{6,8},{8,10},{10,12},{12,14},{14,16},{16,18},{18... | collective-permute-start | bytes 442376 | tf_op jit(solution)/shard_map/ppermute | solution.py:26
  29.2 7.1 %collective-permute-start.13 = (bf16[48,1536]{1,0:T(8,128)(2,1)S(1)}, bf16[48,1536]{1,0:T(8,128)(2,1)S(1)}, u32[]{:S(2)}, u32[]{:S(2)}) collective-permute-start(bf16[48,1536]{1,0:T(8,128)(2,1)S(1)} %collective-permute-done.12), channel_id=1, source_target_pairs={{2,0},{4,2},{6,4},{8,6},{10,8},{12,10},{14,12},{16,14},{18,16},{20... | collective-permute-start | bytes 442376 | tf_op jit(solution)/shard_map/ppermute | solution.py:28
  35.6 7.6 %collective-permute-start.7 = (bf16[48,1536]{1,0:T(8,128)(2,1)}, bf16[48,1536]{1,0:T(8,128)(2,1)S(1)}, u32[]{:S(2)}, u32[]{:S(2)}) collective-permute-start(bf16[48,1536]{1,0:T(8,128)(2,1)} %collective-permute-done.6), channel_id=1, source_target_pairs={{0,2},{2,4},{4,6},{6,8},{8,10},{10,12},{12,14},{14,16},{16,18},{18... | collective-permute-start | bytes 442376 | tf_op jit(solution)/shard_map/ppermute | solution.py:26
  37.0 7.3 %collective-permute-start.14 = (bf16[48,1536]{1,0:T(8,128)(2,1)S(1)}, bf16[48,1536]{1,0:T(8,128)(2,1)S(1)}, u32[]{:S(2)}, u32[]{:S(2)}) collective-permute-start(bf16[48,1536]{1,0:T(8,128)(2,1)S(1)} %collective-permute-done.13), channel_id=1, source_target_pairs={{2,0},{4,2},{6,4},{8,6},{10,8},{12,10},{14,12},{16,14},{18,16},{20... | collective-permute-start | bytes 442376 | tf_op jit(solution)/shard_map/ppermute | solution.py:28
  43.2 7.4 %collective-permute-start.8 = (bf16[48,1536]{1,0:T(8,128)(2,1)S(1)}, bf16[48,1536]{1,0:T(8,128)(2,1)S(1)}, u32[]{:S(2)}, u32[]{:S(2)}) collective-permute-start(bf16[48,1536]{1,0:T(8,128)(2,1)S(1)} %collective-permute-done.7), channel_id=1, source_target_pairs={{0,2},{2,4},{4,6},{6,8},{8,10},{10,12},{12,14},{14,16},{16,18},{18... | collective-permute-start | bytes 442376 | tf_op jit(solution)/shard_map/ppermute | solution.py:26
  44.9 7.4 %collective-permute-start.15 = (bf16[48,1536]{1,0:T(8,128)(2,1)S(1)}, bf16[48,1536]{1,0:T(8,128)(2,1)}, u32[]{:S(2)}, u32[]{:S(2)}) collective-permute-start(bf16[48,1536]{1,0:T(8,128)(2,1)S(1)} %collective-permute-done.14), channel_id=1, source_target_pairs={{2,0},{4,2},{6,4},{8,6},{10,8},{12,10},{14,12},{16,14},{18,16},{20... | collective-permute-start | bytes 442376 | tf_op jit(solution)/shard_map/ppermute | solution.py:28
  50.5 7.5 %collective-permute-start.9 = (bf16[48,1536]{1,0:T(8,128)(2,1)S(1)}, bf16[48,1536]{1,0:T(8,128)(2,1)}, u32[]{:S(2)}, u32[]{:S(2)}) collective-permute-start(bf16[48,1536]{1,0:T(8,128)(2,1)S(1)} %collective-permute-done.8), channel_id=1, source_target_pairs={{0,2},{2,4},{4,6},{6,8},{8,10},{10,12},{12,14},{14,16},{16,18},{18... | collective-permute-start | bytes 442376 | tf_op jit(solution)/shard_map/ppermute | solution.py:26
  52.3 7.7 %collective-permute-start.16 = (bf16[48,1536]{1,0:T(8,128)(2,1)}, bf16[48,1536]{1,0:T(8,128)(2,1)}, u32[]{:S(2)}, u32[]{:S(2)}) collective-permute-start(bf16[48,1536]{1,0:T(8,128)(2,1)} %collective-permute-done.15), channel_id=1, source_target_pairs={{2,0},{4,2},{6,4},{8,6},{10,8},{12,10},{14,12},{16,14},{18,16},{20... | collective-permute-start | bytes 442376 | tf_op jit(solution)/shard_map/ppermute | solution.py:28
  58.0 7.6 %collective-permute-start.10 = (bf16[48,1536]{1,0:T(8,128)(2,1)}, bf16[48,1536]{1,0:T(8,128)(2,1)}, u32[]{:S(2)}, u32[]{:S(2)}) collective-permute-start(bf16[48,1536]{1,0:T(8,128)(2,1)} %collective-permute-done.9), channel_id=1, source_target_pairs={{0,2},{2,4},{4,6},{6,8},{8,10},{10,12},{12,14},{14,16},{16,18},{18... | collective-permute-start | bytes 442376 | tf_op jit(solution)/shard_map/ppermute | solution.py:26
  60.0 7.7 %collective-permute-start.17 = (bf16[48,1536]{1,0:T(8,128)(2,1)}, bf16[48,1536]{1,0:T(8,128)(2,1)}, u32[]{:S(2)}, u32[]{:S(2)}) collective-permute-start(bf16[48,1536]{1,0:T(8,128)(2,1)} %collective-permute-done.16), channel_id=1, source_target_pairs={{2,0},{4,2},{6,4},{8,6},{10,8},{12,10},{14,12},{16,14},{18,16},{20... | collective-permute-start | bytes 442376 | tf_op jit(solution)/shard_map/ppermute | solution.py:28
  65.6 7.6 %collective-permute-start.11 = (bf16[48,1536]{1,0:T(8,128)(2,1)}, bf16[48,1536]{1,0:T(8,128)(2,1)}, u32[]{:S(2)}, u32[]{:S(2)}) collective-permute-start(bf16[48,1536]{1,0:T(8,128)(2,1)} %collective-permute-done.10), channel_id=1, source_target_pairs={{0,2},{2,4},{4,6},{6,8},{8,10},{10,12},{12,14},{14,16},{16,18},{18... | collective-permute-start | bytes 442376 | tf_op jit(solution)/shard_map/ppermute | solution.py:26
  65.8 22.0 %copy-start.44 = (bf16[48,1536]{1,0:T(8,128)(2,1)S(1)}, bf16[48,1536]{1,0:T(8,128)(2,1)}, u32[]{:S(2)}) copy-start(bf16[48,1536]{1,0:T(8,128)(2,1)} %copy-done.43) | copy-start | bytes 442372
  65.9 32.9 %copy-start.17 = (bf16[256,1536]{1,0:T(8,128)(2,1)}, bf16[256,1536]{1,0:T(8,128)(2,1)S(1)}, u32[]{:S(2)}) copy-start(bf16[256,1536]{1,0:T(8,128)(2,1)S(1)} %collective-permute-done) | copy-start | bytes 2359300
  65.9 22.6 %collective-permute-start.1 = (bf16[256,1536]{1,0:T(8,128)(2,1)S(1)}, bf16[256,1536]{1,0:T(8,128)(2,1)S(1)}, u32[]{:S(2)}, u32[]{:S(2)}) collective-permute-start(bf16[256,1536]{1,0:T(8,128)(2,1)S(1)} %collective-permute-done), channel_id=1, source_target_pairs={{0,2},{2,4},{4,6},{6,8},{8,10},{10,12},{12,14},{14,16},{16,18},{18... | collective-permute-start | bytes 2359304 | tf_op jit(solution)/shard_map/ppermute | solution.py:38
  67.7 31.0 %collective-permute-start.18 = (bf16[48,1536]{1,0:T(8,128)(2,1)}, bf16[48,1536]{1,0:T(8,128)(2,1)S(1)}, u32[]{:S(2)}, u32[]{:S(2)}) collective-permute-start(bf16[48,1536]{1,0:T(8,128)(2,1)} %collective-permute-done.17), channel_id=1, source_target_pairs={{2,0},{4,2},{6,4},{8,6},{10,8},{12,10},{14,12},{16,14},{18,16},{20... | collective-permute-start | bytes 442376 | tf_op jit(solution)/shard_map/ppermute | solution.py:28
  88.5 5.4 %collective-permute-start.2 = (bf16[256,1536]{1,0:T(8,128)(2,1)S(1)}, bf16[256,1536]{1,0:T(8,128)(2,1)}, u32[]{:S(2)}, u32[]{:S(2)}) collective-permute-start(bf16[256,1536]{1,0:T(8,128)(2,1)S(1)} %collective-permute-done.1), channel_id=1, source_target_pairs={{0,2},{2,4},{4,6},{6,8},{8,10},{10,12},{12,14},{14,16},{16,18},{18... | collective-permute-start | bytes 2359304 | tf_op jit(solution)/shard_map/ppermute | solution.py:38
  93.9 9.4 %collective-permute-start.3 = (bf16[256,1536]{1,0:T(8,128)(2,1)}, bf16[256,1536]{1,0:T(8,128)(2,1)}, u32[]{:S(2)}, u32[]{:S(2)}) collective-permute-start(bf16[256,1536]{1,0:T(8,128)(2,1)} %collective-permute-done.2), channel_id=1, source_target_pairs={{0,2},{2,4},{4,6},{6,8},{8,10},{10,12},{12,14},{14,16},{16,18},{18... | collective-permute-start | bytes 2359304 | tf_op jit(solution)/shard_map/ppermute | solution.py:38
  144.3 165.2 %reduce-scatter.5.cloned.1.call-start = ((), (), s32[]{:S(2)}) async-start(), calls=%async_computation.3 | async-start | bytes 2506752 | tf_op jit(solution)/shard_map/reduce_scatter | solution.py:107
  168.2 14.1 %collective-permute-start.19 = (f32[256,1536]{1,0:T(8,128)}, f32[256,1536]{1,0:T(8,128)}, u32[]{:S(2)}, u32[]{:S(2)}) collective-permute-start(f32[256,1536]{1,0:T(8,128)} %pad_maximum_fusion), channel_id=1, source_target_pairs={{2,0},{4,2},{6,4},{8,6},{10,8},{12,10},{14,12},{16,14},{18,16},{20... | collective-permute-start | bytes 4718600 | tf_op jit(solution)/shard_map/ppermute | solution.py:38
  185.1 24.4 %collective-permute-start.20 = (f32[256,1536]{1,0:T(8,128)}, f32[256,1536]{1,0:T(8,128)}, u32[]{:S(2)}, u32[]{:S(2)}) collective-permute-start(f32[256,1536]{1,0:T(8,128)} %maximum_add_fusion), channel_id=1, source_target_pairs={{2,0},{4,2},{6,4},{8,6},{10,8},{12,10},{14,12},{16,14},{18,16},{20... | collective-permute-start | bytes 4718600 | tf_op jit(solution)/shard_map/ppermute | solution.py:38
  212.8 19.2 %collective-permute-start.21 = (f32[256,1536]{1,0:T(8,128)}, f32[256,1536]{1,0:T(8,128)}, u32[]{:S(2)}, u32[]{:S(2)}) collective-permute-start(f32[256,1536]{1,0:T(8,128)} %maximum_add_fusion.1), channel_id=1, source_target_pairs={{2,0},{4,2},{6,4},{8,6},{10,8},{12,10},{14,12},{16,14},{18,16},{20... | collective-permute-start | bytes 4718600 | tf_op jit(solution)/shard_map/ppermute | solution.py:38
  234.9 22.4 %collective-permute-start.22 = (f32[256,1536]{1,0:T(8,128)}, f32[256,1536]{1,0:T(8,128)}, u32[]{:S(2)}, u32[]{:S(2)}) collective-permute-start(f32[256,1536]{1,0:T(8,128)} %maximum_add_fusion.2), channel_id=1, source_target_pairs={{2,0},{4,2},{6,4},{8,6},{10,8},{12,10},{14,12},{16,14},{18,16},{20... | collective-permute-start | bytes 4718600 | tf_op jit(solution)/shard_map/ppermute | solution.py:38
  242.3 67.2 %copy-start.1 = (bf16[1,256,1536]{2,1,0:T(8,128)(2,1)S(1)}, bf16[1,256,1536]{2,1,0:T(8,128)(2,1)}, u32[]{:S(2)}) copy-start(bf16[1,256,1536]{2,1,0:T(8,128)(2,1)} %param.9) | copy-start | bytes 2359300
  (47 other events, 189.1 us)
Sparse Core Ops, SparseCore 0:
  144.4 68.8 reduce-scatter.2
  224.3 85.1 reduce-scatter.4
